TPU v7x, 256 devices: a whole 4x4x8 slice. The times are simulated.
256 devices in a mesh: dp: 16 (over y, x_lo, core), ctx: 8 (over z), tp: 2 (over x_hi).
Axes of the slice: x: 4 (x_hi: 2, x_lo: 2; x = x_hi * 2 + x_lo), y: 4, z: 8, core: 2. Of those that a mesh axis runs over, the one named last changes fastest.
Arguments:
- tokens: bfloat16 [16, 2048, 8192], P('dp', 'ctx', 'tp'), may hold values from -6 to 6
- queries: bfloat16 [16, 2048, 8192], P('dp', 'ctx', 'tp'), may hold values from -180 to 180
- k_weight: bfloat16 [8192, 512], P('dp', 'tp'), may hold values from -0.0625 to 0.0625
- v_weight: bfloat16 [8192, 512], P('dp', 'tp'), may hold values from -0.0625 to 0.0625
- doc_blocks: int32 [16, 16], P('dp', 'ctx'), may hold values from 0 to 3, never falling along the last dimension, each value on 1 to 8 neighbouring positions
Outputs:
- context: bfloat16 [16, 2048, 8192], P('dp', 'ctx', 'tp')
Inputs may be any that keep to these rules, and one draw needn't show every extreme that they name: `doc_blocks`: along each sequence the document numbers never fall; each document covers 1 to 8 whole blocks, one exactly 8.
All inputs are finite; a program needn't handle non-finite values.
Results may differ from a plain program's by a relative error of at most 0.012.
The roundings to bfloat16 on the way count: a program that leaves them out, or rounds other values in their place, can miss the bound.
Values may be sent and summed in bfloat16 or wider, within the bound.
No kernel may reach another device: no remote copies, remote signals or barrier semaphores. Data moves between devices by JAX's collectives and lax.ppermute only.
A program may use at most 192 MiB of HBM per device.

v0:
```python
import math

import jax
import jax.numpy as jnp
from jax import lax
from jax.sharding import PartitionSpec as P

HD = 128
BLOCK = 128


ROPE_BASE = 500000.0
YARN_FACTOR = 16.0
PRETRAIN_CONTEXT = 8192.0
BETA_FAST = 32.0
BETA_SLOW = 1.0
ATTN_FACTOR = (1.0 + 0.1 * math.log(16.0)) ** 2
MASKED_SCORE = -1e30


def yarn_tables(positions):
    counter = jnp.arange(HD // 2, dtype=jnp.float32)
    base_freq = ROPE_BASE ** (-2.0 * counter / HD)
    wave_ratio = PRETRAIN_CONTEXT * base_freq / (2.0 * math.pi)
    ramp_value = jnp.clip((wave_ratio - BETA_SLOW) / (BETA_FAST - BETA_SLOW), 0.0, 1.0)
    frequency = ramp_value * base_freq + (1.0 - ramp_value) * base_freq / YARN_FACTOR
    angles = positions.astype(jnp.float32)[:, None] * frequency[None, :]
    cosine = jnp.cos(angles)
    sine_table = jnp.sin(angles)
    return (
        jnp.concatenate([cosine, cosine], axis=-1),
        jnp.concatenate([sine_table, sine_table], axis=-1),
    )


def rotate(vectors, cosine, sine_table):
    half_width = vectors.shape[-1] // 2
    lower_half = vectors[..., :half_width]
    upper_half = vectors[..., half_width:]
    turned = jnp.concatenate([-upper_half, lower_half], axis=-1)
    return vectors * cosine[:, None, :] + turned * sine_table[:, None, :]


def collect_features(local_tokens):
    return lax.all_gather(local_tokens, "tp", axis=1, tiled=True)


def body(tokens, queries, k_weight, v_weight, doc_blocks):
    local_tokens = tokens[0]
    row_count = local_tokens.shape[0]
    ctx_rank = lax.axis_index("ctx")
    all_docs = lax.all_gather(doc_blocks[0], "ctx", axis=0, tiled=True)
    kv_width = k_weight.shape[1]
    kv_heads = kv_width // HD
    whole = collect_features(local_tokens)
    pieces = (
        lax.all_gather(k_weight, "dp", axis=0, tiled=True),
        lax.all_gather(v_weight, "dp", axis=0, tiled=True),
    )
    height = pieces[0].shape[0]
    key_proj = jnp.dot(whole, pieces[0], preferred_element_type=jnp.float32)
    value_proj = jnp.dot(whole, pieces[1], preferred_element_type=jnp.float32)
    positions = ctx_rank * row_count + jnp.arange(row_count, dtype=jnp.int32)
    cosine, sine_table = yarn_tables(positions)
    key_rows = (
        rotate(key_proj.reshape(row_count, kv_heads, HD), cosine, sine_table)
        .reshape(row_count, kv_width)
        .astype(jnp.bfloat16)
    )
    value_rows = value_proj.astype(jnp.bfloat16)
    local_queries = queries[0]
    query_heads = local_queries.shape[1] // HD
    group_size = query_heads // kv_heads
    query_rot = (
        (
            rotate(
                local_queries.astype(jnp.float32).reshape(row_count, query_heads, HD),
                cosine,
                sine_table,
            )
            * (ATTN_FACTOR / math.sqrt(HD))
        )
        .reshape(row_count, query_heads * HD)
        .astype(jnp.bfloat16)
    )
    token_docs = jnp.repeat(all_docs, BLOCK)
    query_total = query_rot.shape[0]
    query_docs = token_docs[positions]
    grouped = query_rot.reshape(query_total, kv_heads, group_size, HD)
    start_max = jnp.full((kv_heads, group_size, query_total), MASKED_SCORE, jnp.float32)
    start_sum = jnp.zeros((kv_heads, group_size, query_total), jnp.float32)
    start_acc = jnp.zeros((kv_heads, group_size, query_total, HD), jnp.float32)
    key_piece = lax.all_gather(key_rows, "ctx", axis=0, tiled=True)
    value_piece = lax.all_gather(value_rows, "ctx", axis=0, tiled=True)
    height = key_piece.shape[0]
    key_pos = jnp.arange(height, dtype=jnp.int32)
    visible = (key_pos[None, :] <= positions[:, None]) & (
        token_docs[None, :] == query_docs[:, None]
    )

    def update(state):
        running_max, running_sum, running_acc = state
        scores = jnp.einsum(
            "qkgd,nkd->kgqn",
            grouped,
            key_piece.reshape(height, kv_heads, HD),
            preferred_element_type=jnp.float32,
        )
        scores = jnp.where(visible, scores, MASKED_SCORE)
        new_max = jnp.maximum(running_max, jnp.max(scores, axis=-1))
        weights = jnp.where(visible, jnp.exp(scores - new_max[..., None]), 0.0)
        new_sum = jnp.sum(weights, axis=-1)
        new_acc = jnp.einsum(
            "kgqn,nkd->kgqd",
            weights.astype(jnp.bfloat16),
            value_piece.reshape(height, kv_heads, HD),
            preferred_element_type=jnp.float32,
        )
        return (new_max, new_sum, new_acc)

    def unchanged(state):
        return state

    final_max, final_sum, final_acc = lax.cond(
        jnp.any(visible), update, unchanged, (start_max, start_sum, start_acc)
    )
    attended = final_acc / final_sum[..., None]
    context = (
        attended.transpose(2, 0, 1, 3).reshape(query_total, query_heads * HD).astype(jnp.bfloat16)
    )
    return context[None]


def solution(mesh):
    placed = (
        P("dp", "ctx", "tp"),
        P("dp", "ctx", "tp"),
        P("dp", "tp"),
        P("dp", "tp"),
        P("dp", "ctx"),
    )
    return jax.shard_map(
        body, mesh=mesh, in_specs=placed, out_specs=P("dp", "ctx", "tp"), check_vma=False
    )
```

profile of v0, /device:TPU:100, one launch (start us, length us, event | category | flops | bytes accessed | tf_op | source)
XLA Modules:
  0.0 325.7 jit_solution(8934308022742542548)
XLA Ops:
  6.5 0.7 all-gather.16.cloned.1.call-update
  9.2 62.7 %all-gather.16.cloned.1.call-done = bf16[1,256,8192]{2,1,0:T(8,128)(2,1)} async-done(((bf16[1,256,4096]{2,1,0:T(8,128)(2,1)}), bf16[1,256,8192]{2,1,0:T(8,128)(2,1)}) %all-gather.16.cloned.1.call-update) | async-done | bytes 4194320 | tf_op jit(solution)/shard_map/all_gather | solution.py:45
  71.9 43.2 %all-gather.8.cloned.1.call-done = bf16[8192,256]{1,0:T(8,128)(2,1)} async-done(((bf16[512,256]{1,0:T(8,128)(2,1)}), bf16[8192,256]{1,0:T(8,128)(2,1)}) %all-gather.8.cloned.1.call-update) | async-done | bytes 4194320 | tf_op jit(solution)/shard_map/all_gather | solution.py:57
  115.0 5.2 %fusion.11 = f32[256,256]{0,1:T(8,128)S(1)} fusion(bf16[8192,256]{1,0:T(8,128)(2,1)} %all-gather.8.cloned.1.call-done, bf16[1,256,8192]{2,1,0:T(8,128)(2,1)} %all-gather.16.cloned.1.call-done), kind=kOutput, calls=%fused_computation.15 | convolution fusion | flops 1073741824 | bytes 8650752 | tf_op jit(solution)/shard_map/dot_general | solution.py:61
  122.4 34.4 %all-gather.12.cloned.1.call-done = bf16[8192,256]{1,0:T(8,128)(2,1)} async-done(((bf16[512,256]{1,0:T(8,128)(2,1)}), bf16[8192,256]{1,0:T(8,128)(2,1)}) %all-gather.12.cloned.1.call-update) | async-done | bytes 4194320 | tf_op jit(solution)/shard_map/all_gather | solution.py:58
  156.7 5.4 %fusion.15 = bf16[256,256]{1,0:T(8,128)(2,1)} fusion(bf16[8192,256]{1,0:T(8,128)(2,1)} %all-gather.12.cloned.1.call-done, bf16[1,256,8192]{2,1,0:T(8,128)(2,1)} %all-gather.16.cloned.1.call-done), kind=kOutput, calls=%fused_computation.23 | convolution fusion | flops 1073807360 | bytes 8519680 | tf_op jit(solution)/shard_map/dot_general | solution.py:62
  162.1 3.3 %copy.18 = bf16[1,256,4096]{1,2,0:T(8,128)(2,1)S(1)} copy(bf16[1,256,4096]{2,1,0:T(8,128)(2,1)} %param.8) | data formatting | bytes 4194304 | tf_op args[1]
  165.4 2.3 convert_element_type.65
  167.7 12.8 %all-reduce = s32[16]{0:T(128)S(1)} all-reduce(s32[16]{0:T(128)S(1)} %bitcast_dynamic-update-slice_fusion), channel_id=2, replica_groups=mesh['dp'=16,'ctx'=8,'tp'=2] {'ctx'}, use_global_device_ids=true, to_apply=%add | all-reduce | flops 16 | bytes 128
  180.6 1.7 gather_fusion
  182.3 1.3 fusion.14
  184.1 2.5 slice_negate_fusion
  187.2 1.7 copy-done
  188.9 1.1 multiply_convert_fusion
  189.9 7.7 %all-gather.10.cloned.1.call-done = bf16[2048,256]{0,1:T(8,128)(2,1)} async-done(((bf16[256,256]{0,1:T(8,128)(2,1)}), bf16[2048,256]{0,1:T(8,128)(2,1)}) %all-gather.10.cloned.1.call-update) | async-done | bytes 1048592 | tf_op jit(solution)/shard_map/all_gather | solution.py:93
  197.6 39.0 %all-gather.14.cloned.1.call-done = bf16[2048,256]{1,0:T(8,128)(2,1)} async-done(((bf16[256,256]{1,0:T(8,128)(2,1)}), bf16[2048,256]{1,0:T(8,128)(2,1)}) %all-gather.14.cloned.1.call-update) | async-done | bytes 1048592 | tf_op jit(solution)/shard_map/all_gather | solution.py:94
  236.6 76.0 %conditional.1 = (f32[2,16,256]{2,1,0:T(8,128)S(1)}, f32[2,16,256,128]{3,2,1,0:T(8,128)}) conditional(s32[]{:T(128)} %convert_element_type.53, () %tuple.13, (pred[256,2048]{0,1:T(8,128)(4,1)S(1)}, bf16[2048,256]{0,1:T(8,128)(2,1)}, bf16[256,2,16,128]{0,3,2,1:T(8,128)(2,1)S(1)}, bf16[2048,256]{1,0:T(8,128)(2,1)}) %tuple.14), branch_computations={%region_1.2_spmd, %region_2.5_spmd} | conditional | flops 8757698560 | bytes 213581840 | solution.py:124
  236.6 24.4 %fusion = (f32[2,16,256]{2,1,0:T(8,128)S(1)}, f32[2,2048,256,16]{2,1,3,0:T(8,128)}) fusion(pred[256,2048]{0,1:T(8,128)(4,1)S(1)} %get-tuple-element.13, bf16[2048,2,128,1]{0,2,3,1:T(8,128)(2,1)} %bitcast.55, bf16[256,2,16,128]{0,3,2,1:T(8,128)(2,1)S(1)} %get-tuple-element.27), kind=kOutput, calls=%fused_computation.3 | convolution fusion | flops 4328513536 | bytes 70811648 | tf_op jit(solution)/shard_map/cond/branch_1_fun/qkgd,nkd->kgqn/dot_general | solution.py:103
  261.0 1.3 reshape.84
  262.3 28.7 %fusion.3 = f32[2,16,256,128]{3,2,1,0:T(8,128)} fusion(f32[2,2048,256,16]{2,1,3,0:T(8,128)} %get-tuple-element.30, f32[2,16,256]{2,1,0:T(8,128)S(1)} %broadcast_maximum_fusion, pred[256,2048]{0,1:T(8,128)(4,1)S(1)} %get-tuple-element.13, bf16[2048,2,128,1]{2,1,0,3:T(2,128)(2,1)S(1)} %bitcast.54), kind=kOutput, calls=%fused_computation.6 | convolution fusion | flops 4362076160 | bytes 72908800 | tf_op jit(solution)/shard_map/cond/branch_1_fun/kgqn,nkd->kgqd/dot_general | solution.py:113
  291.0 21.6 %fusion.2 = f32[2,16,256]{2,1,0:T(8,128)S(1)} fusion(f32[2,2048,256,16]{2,1,3,0:T(8,128)} %get-tuple-element.30, f32[2,16,256]{2,1,0:T(8,128)S(1)} %broadcast_maximum_fusion, pred[256,2048]{0,1:T(8,128)(4,1)S(1)} %get-tuple-element.13), kind=kLoop, calls=%fused_computation.5 | loop fusion | flops 67100672 | bytes 67698688 | tf_op jit(solution)/shard_map/cond/branch_1_fun/reduce_sum | solution.py:112
  312.6 2.9 fusion.13
  315.5 1.4 copy.21
  316.9 2.3 convert_element_type.64
  (30 shorter events, 3.9 us)
Async XLA Ops:
  6.5 65.3 %all-gather.16.cloned.1.call-start = ((), (), s32[]{:S(2)}) async-start(), calls=%async_computation.4 | async-start | bytes 6291456 | tf_op jit(solution)/shard_map/all_gather | solution.py:45
  7.3 107.8 %all-gather.8.cloned.1.call-start = ((), (), s32[]{:S(2)}) async-start(), calls=%async_computation | async-start | bytes 4456448 | tf_op jit(solution)/shard_map/all_gather | solution.py:57
  8.0 148.7 %all-gather.12.cloned.1.call-start = ((), (), s32[]{:S(2)}) async-start(), calls=%async_computation.2 | async-start | bytes 4456448 | tf_op jit(solution)/shard_map/all_gather | solution.py:58
  8.7 188.9 %all-gather.10.cloned.1.call-start = ((), (), s32[]{:S(2)}) async-start(), calls=%async_computation.1 | async-start | bytes 1179648 | tf_op jit(solution)/shard_map/all_gather | solution.py:93
  9.2 111.9 %copy-start.2 = (u32[256]{0:T(256)S(1)}, u32[256]{0:T(256)}, u32[]{:S(2)}) copy-start(u32[256]{0:T(256)} %constant.56) | copy-start | bytes 3076
  9.2 113.1 %copy-start.1 = (s32[1,2]{1,0:T(1,128)S(1)}, s32[1,2]{1,0:T(1,128)}, u32[]{:S(2)}) copy-start(s32[1,2]{1,0:T(1,128)} %param.11) | copy-start | bytes 28
  121.0 115.5 %all-gather.14.cloned.1.call-start = ((), (), s32[]{:S(2)}) async-start(), calls=%async_computation.3 | async-start | bytes 1179648 | tf_op jit(solution)/shard_map/all_gather | solution.py:94
  186.7 2.2 copy-start
Sparse Core Ops, SparseCore 0:
  9.1 62.6 all-gather.15
  73.7 41.2 all-gather.7
  116.9 39.7 all-gather.11
  158.3 39.2 all-gather.9
  199.2 37.2 all-gather.13
where the time goes:
time: 328 us; the launch traced here: 326 us
  waiting for transfers between devices  189 us (58%)
  matrix products  63.7 us (19%)
  other arithmetic  33.2 us (10%)
  between operations  14.4 us (4%)
  blocking collectives  12.8 us (4%)
  local copies, waits for them, and re-layouts  12.5 us (4%)
    all_gather x1, waiting for transfers between devices, collect_features(): return lax.all_gather(local_tokens, 'tp', axis=1, tiled=True)  62.7 us
    all_gather x1, waiting for transfers between devices, body(): lax.all_gather(k_weight, 'dp', axis=0, tiled=True)  43.2 us
    all_gather x1, waiting for transfers between devices, body(): value_piece = lax.all_gather(value_rows, 'ctx', axis=0, tiled=True)  39 us
    all_gather x1, waiting for transfers between devices, body(): lax.all_gather(v_weight, 'dp', axis=0, tiled=True)  34.4 us
    dot_general x1, matrix products, update(): jnp.einsum('kgqn,nkd->kgqd', weights.astype(jnp.bfloat16), value_piece.re...  28.7 us
    dot_general x1, matrix products, update(): jnp.einsum('qkgd,nkd->kgqn', grouped, key_piece.reshape(height, kv_heads,...  24.4 us
    reduce_sum x1, other arithmetic, update(): new_sum = jnp.sum(weights, axis=-1)  21.6 us
    unnamed x1, blocking collectives  12.8 us
  transfers between devices with their start and end apart: 5, of which 5 were waited for; matrix products, arithmetic and copies ran while one was open for 8% of the time, Pallas kernels for 0%

commit v1 on v0

v1 whole, which is shorter than its diff:
```python
import math

import jax
import jax.numpy as jnp
from jax import lax
from jax.sharding import PartitionSpec as P

HD = 128
BLOCK = 128
LOOKBACK = 7


ROPE_BASE = 500000.0
YARN_FACTOR = 16.0
PRETRAIN_CONTEXT = 8192.0
BETA_FAST = 32.0
BETA_SLOW = 1.0
ATTN_FACTOR = (1.0 + 0.1 * math.log(16.0)) ** 2
MASKED_SCORE = -1e30


def yarn_tables(positions):
    counter = jnp.arange(HD // 2, dtype=jnp.float32)
    base_freq = ROPE_BASE ** (-2.0 * counter / HD)
    wave_ratio = PRETRAIN_CONTEXT * base_freq / (2.0 * math.pi)
    ramp_value = jnp.clip((wave_ratio - BETA_SLOW) / (BETA_FAST - BETA_SLOW), 0.0, 1.0)
    frequency = ramp_value * base_freq + (1.0 - ramp_value) * base_freq / YARN_FACTOR
    angles = positions.astype(jnp.float32)[:, None] * frequency[None, :]
    cosine = jnp.cos(angles)
    sine_table = jnp.sin(angles)
    return (
        jnp.concatenate([cosine, cosine], axis=-1),
        jnp.concatenate([sine_table, sine_table], axis=-1),
    )


def rotate(vectors, cosine, sine_table):
    half_width = vectors.shape[-1] // 2
    lower_half = vectors[..., :half_width]
    upper_half = vectors[..., half_width:]
    turned = jnp.concatenate([-upper_half, lower_half], axis=-1)
    return vectors * cosine[:, None, :] + turned * sine_table[:, None, :]


def shift_pairs(count, step):
    return [(i, i + step) for i in range(count - step)]


def make_body(n_ctx):
    def body(tokens, queries, k_weight, v_weight, doc_blocks):
        local_tokens = tokens[0]
        row_count, feat_half = local_tokens.shape
        ctx_rank = lax.axis_index("ctx")
        tp_rank = lax.axis_index("tp")
        kv_width = k_weight.shape[1]
        kv_heads = kv_width // HD

        joined = jnp.concatenate([k_weight, v_weight], axis=1)
        weights = lax.all_gather(joined, "dp", axis=0, tiled=True)
        weights = weights.reshape(2, feat_half, 2 * kv_width)
        partner_tokens = lax.ppermute(local_tokens, "tp", [(0, 1), (1, 0)])
        proj = jnp.dot(local_tokens, weights[tp_rank], preferred_element_type=jnp.float32)
        proj = proj + jnp.dot(
            partner_tokens, weights[1 - tp_rank], preferred_element_type=jnp.float32
        )

        positions = ctx_rank * row_count + jnp.arange(row_count, dtype=jnp.int32)
        cosine, sine_table = yarn_tables(positions)
        key_rows = (
            rotate(proj[:, :kv_width].reshape(row_count, kv_heads, HD), cosine, sine_table)
            .reshape(row_count, kv_width)
            .astype(jnp.bfloat16)
        )
        value_rows = proj[:, kv_width:].astype(jnp.bfloat16)
        kv_rows = jnp.concatenate([key_rows, value_rows], axis=1)

        local_docs = doc_blocks[0]
        blocks_here = row_count // BLOCK
        window_kv = []
        window_docs = []
        need = LOOKBACK
        step = 1
        while need > 0:
            take = min(need, blocks_here)
            pairs = shift_pairs(n_ctx, step)
            window_kv.insert(0, lax.ppermute(kv_rows[(blocks_here - take) * BLOCK:], "ctx", pairs))
            window_docs.insert(0, lax.ppermute(local_docs[blocks_here - take:], "ctx", pairs))
            need -= take
            step += 1
        window_kv.append(kv_rows)
        window_docs.append(local_docs)
        kv_all = jnp.concatenate(window_kv, axis=0)
        key_docs = jnp.repeat(jnp.concatenate(window_docs, axis=0), BLOCK)
        height = kv_all.shape[0]
        key_pos = ctx_rank * row_count - (height - row_count) + jnp.arange(height, dtype=jnp.int32)

        local_queries = queries[0]
        query_heads = local_queries.shape[1] // HD
        group_size = query_heads // kv_heads
        query_rot = (
            (
                rotate(
                    local_queries.astype(jnp.float32).reshape(row_count, query_heads, HD),
                    cosine,
                    sine_table,
                )
                * (ATTN_FACTOR / math.sqrt(HD))
            )
            .astype(jnp.bfloat16)
            .reshape(row_count, kv_heads, group_size, HD)
        )
        query_docs = jnp.repeat(local_docs, BLOCK)
        visible = (
            (key_pos[None, :] <= positions[:, None])
            & (key_pos[None, :] >= 0)
            & (key_docs[None, :] == query_docs[:, None])
        )
        keys = kv_all[:, :kv_width].reshape(height, kv_heads, HD)
        values = kv_all[:, kv_width:].reshape(height, kv_heads, HD)
        scores = jnp.einsum("qkgd,nkd->kgqn", query_rot, keys, preferred_element_type=jnp.float32)
        scores = jnp.where(visible, scores, MASKED_SCORE)
        row_max = jnp.max(scores, axis=-1)
        probs = jnp.where(visible, jnp.exp(scores - row_max[..., None]), 0.0)
        row_sum = jnp.sum(probs, axis=-1)
        mixed = jnp.einsum(
            "kgqn,nkd->kgqd", probs.astype(jnp.bfloat16), values, preferred_element_type=jnp.float32
        )
        attended = mixed / row_sum[..., None]
        context = (
            attended.transpose(2, 0, 1, 3).reshape(row_count, query_heads * HD).astype(jnp.bfloat16)
        )
        return context[None]

    return body


def solution(mesh):
    placed = (
        P("dp", "ctx", "tp"),
        P("dp", "ctx", "tp"),
        P("dp", "tp"),
        P("dp", "tp"),
        P("dp", "ctx"),
    )
    return jax.shard_map(
        make_body(mesh.shape["ctx"]),
        mesh=mesh,
        in_specs=placed,
        out_specs=P("dp", "ctx", "tp"),
        check_vma=False,
    )
```

time: 328 us -> 202 us (0.62)
  waiting for transfers between devices: 189 us -> 98.4 us
  other arithmetic: 33.2 us -> 6.23 us
  starting transfers between devices: 0.16 us -> 24 us
  matrix products: 63.7 us -> 40.3 us
  blocking collectives: 12.8 us -> 0 us
  local copies, waits for them, and re-layouts: 12.5 us -> 18.7 us
    all_gather x5 -> x1, waiting for transfers between devices: 187 us -> 64 us  [body(): weights = lax.all_gather(joined, 'dp', axis=0, tiled=True)]
    dot_general x4 -> x3, matrix products: 63.7 us -> 17.6 us  [the longest x1 9.26 us: body(): jnp.einsum('kgqn,nkd->kgqd', probs.astype(jnp.bfloat16), values, preferre...]
    ppermute x0 -> x9, waiting for transfers between devices: none -> 34.4 us  [the longest x4 34.3 us: body(): lax.ppermute(kv_rows[(blocks_here - take) * BLOCK:], 'ctx', pairs)]
    ppermute x0 -> x9, starting transfers between devices: none -> 24 us  [the longest x4 12.1 us: body(): lax.ppermute(local_docs[blocks_here - take:], 'ctx', pairs)]
    sub x0 -> x1, matrix products: none -> 22.7 us  [body(): probs = jnp.where(visible, jnp.exp(scores - row_max[..., None]), 0.0)]
    reduce_sum x1 -> x0, other arithmetic: 21.6 us -> none  [update(): new_sum = jnp.sum(weights, axis=-1)]
    unnamed x1 -> x0, blocking collectives: 12.8 us -> none
    concatenate x0 -> x5, local copies, waits for them, and re-layouts: none -> 7.53 us  [the longest x2 6.69 us: rotate(): turned = jnp.concatenate([-upper_half, lower_half], axis=-1)]
  transfers between devices with their start and end apart: 5 -> 10, of which waited for: 5 -> 4; matrix products, arithmetic and copies ran while one was open for 8% -> 11% of each run, Pallas kernels for 0% -> 0%
where the time goes in v1:
time: 202 us; the launch traced here: 201 us
  waiting for transfers between devices  98.4 us (49%)
  matrix products  40.3 us (20%)
  starting transfers between devices  24 us (12%)
  local copies, waits for them, and re-layouts  18.7 us (9%)
  between operations  13.7 us (7%)
  other arithmetic  6.23 us (3%)
    all_gather x1, waiting for transfers between devices, body(): weights = lax.all_gather(joined, 'dp', axis=0, tiled=True)  64 us
    ppermute x4, waiting for transfers between devices, body(): lax.ppermute(kv_rows[(blocks_here - take) * BLOCK:], 'ctx', pairs)  34.3 us
    sub x1, matrix products, body(): probs = jnp.where(visible, jnp.exp(scores - row_max[..., None]), 0.0)  22.7 us
    ppermute x4, starting transfers between devices, body(): lax.ppermute(local_docs[blocks_here - take:], 'ctx', pairs)  12.1 us
    ppermute x4, starting transfers between devices, body(): lax.ppermute(kv_rows[(blocks_here - take) * BLOCK:], 'ctx', pairs)  11.4 us
    dot_general x1, matrix products, body(): jnp.einsum('kgqn,nkd->kgqd', probs.astype(jnp.bfloat16), values, preferre...  9.26 us
    concatenate x2, local copies, waits for them, and re-layouts, rotate(): turned = jnp.concatenate([-upper_half, lower_half], axis=-1)  6.69 us
    dot_general x1, matrix products, body(): jnp.dot(partner_tokens, weights[1 - tp_rank], preferred_element_type=jnp....  4.17 us
  transfers between devices with their start and end apart: 10, of which 4 were waited for; matrix products, arithmetic and copies ran while one was open for 11% of the time, Pallas kernels for 0%

profile of v1, /device:TPU:100, one launch (start us, length us, event | category | flops | bytes accessed | tf_op | source)
XLA Modules:
  0.0 201.4 jit_solution(7957632940242237227)
XLA Ops:
  6.5 2.0 pad_maximum_fusion
  8.6 5.0 %collective-permute-start.3 = (s32[2]{0:T(128)}, s32[2]{0:T(128)S(1)}, u32[]{:S(2)}, u32[]{:S(2)}) collective-permute-start(s32[2]{0:T(128)} %bitcast.76), channel_id=1, source_target_pairs={{0,2},{2,4},{4,6},{6,8},{8,10},{10,12},{12,14},{1,3},{3,5},{5,7},{... | collective-permute-start | bytes 32 | tf_op jit(solution)/shard_map/ppermute | solution.py:87
  13.6 3.4 %collective-permute-start.2 = (s32[2]{0:T(128)}, s32[2]{0:T(128)S(1)}, u32[]{:S(2)}, u32[]{:S(2)}) collective-permute-start(s32[2]{0:T(128)} %bitcast.77), channel_id=1, source_target_pairs={{0,4},{2,6},{4,8},{6,10},{8,12},{10,14},{1,5},{3,7},{5,9},{7,11},{... | collective-permute-start | bytes 32 | tf_op jit(solution)/shard_map/ppermute | solution.py:87
  17.0 1.9 collective-permute-start.1
  18.9 1.3 slice.34
  20.2 1.8 collective-permute-start
  23.5 3.0 %copy.17 = f32[1,256,4096]{1,2,0:T(8,128)} copy(bf16[1,256,4096]{2,1,0:T(8,128)(2,1)S(1)} %copy-done.1) | data formatting | bytes 6291456 | tf_op jit(solution)/shard_map/convert_element_type | solution.py:103
  27.0 2.8 %copy.28 = f32[32,8,32,128]{3,2,1,0:T(8,128)} copy(f32[32,8,32,128]{3,1,2,0:T(8,128)S(1)} %convert_bitcast_fusion) | data formatting | bytes 8388608
  30.7 1.7 slice_negate_fusion
  32.4 3.9 %copy.19 = f32[256,2,16,64]{3,0,2,1:T(8,128)} copy(f32[256,2,16,64]{0,3,2,1:T(8,128)} %bitcast.70) | data formatting | bytes 4194304 | tf_op jit(solution)/shard_map/concatenate | solution.py:41
  36.3 2.8 %copy.18 = f32[256,2,16,64]{3,0,2,1:T(8,128)} copy(f32[256,2,16,64]{0,3,2,1:T(8,128)S(1)} %bitcast.69) | data formatting | bytes 4194304 | tf_op jit(solution)/shard_map/concatenate | solution.py:41
  40.0 64.0 %all-gather.2.cloned.1.call-done = bf16[8192,512]{1,0:T(8,128)(2,1)} async-done(((bf16[512,512]{1,0:T(8,128)(2,1)}), bf16[8192,512]{1,0:T(8,128)(2,1)}) %all-gather.2.cloned.1.call-update) | async-done | bytes 8388624 | tf_op jit(solution)/shard_map/all_gather | solution.py:59
  104.0 4.2 %fusion.15 = f32[512,256]{1,0:T(8,128)S(1)} fusion(bf16[2,4096,512]{2,1,0:T(8,128)(2,1)} %bitcast.81, s32[]{:T(128)S(6)} %select_n.13, bf16[1,256,4096]{2,1,0:T(8,128)(2,1)} %param.5), kind=kOutput, calls=%fused_computation.18 | convolution fusion | flops 1073741824 | bytes 6815748 | tf_op jit(solution)/shard_map/dot_general | solution.py:62
  108.2 4.2 %fusion.24 = f32[256,512]{0,1:T(8,128)S(1)} fusion(f32[512,256]{1,0:T(8,128)S(1)} %fusion.15, bf16[256,4096]{1,0:T(8,128)(2,1)} %collective-permute-done.4, bf16[2,4096,512]{2,1,0:T(8,128)(2,1)} %bitcast.82, s32[]{:T(128)S(6)} %select_n.14), kind=kOutput, calls=%fused_computation.25 | convolution fusion | flops 1073872896 | bytes 7340036 | tf_op jit(solution)/shard_map/dot_general | solution.py:63
  112.6 5.5 %collective-permute-start.7 = (bf16[256,512]{0,1:T(8,128)(2,1)S(1)}, bf16[256,512]{0,1:T(8,128)(2,1)S(1)}, u32[]{:S(2)}, u32[]{:S(2)}) collective-permute-start(bf16[256,512]{0,1:T(8,128)(2,1)S(1)} %pad_maximum_fusion.1), channel_id=1, source_target_pairs={{0,4},{2,6},{4,8},{6,10},{8,12},{10,14},{1,5},{3,7},{5,9},{7,11},{... | collective-permute-start | bytes 786440 | tf_op jit(solution)/shard_map/ppermute | solution.py:86
  118.0 1.9 collective-permute-start.6
  120.0 1.3 collective-permute-start.5
  121.3 1.1 compare_and_fusion
  122.3 2.7 %collective-permute-start.8 = (bf16[256,512]{0,1:T(8,128)(2,1)S(1)}, bf16[256,512]{0,1:T(8,128)(2,1)S(1)}, u32[]{:S(2)}, u32[]{:S(2)}) collective-permute-start(bf16[256,512]{0,1:T(8,128)(2,1)S(1)} %pad_maximum_fusion.1), channel_id=1, source_target_pairs={{0,2},{2,4},{4,6},{6,8},{8,10},{10,12},{12,14},{1,3},{3,5},{5,7},{... | collective-permute-start | bytes 786440 | tf_op jit(solution)/shard_map/ppermute | solution.py:86
  125.1 11.1 %collective-permute-done.6 = bf16[256,512]{0,1:T(8,128)(2,1)S(1)} collective-permute-done((bf16[256,512]{0,1:T(8,128)(2,1)S(1)}, bf16[256,512]{0,1:T(8,128)(2,1)S(1)}, u32[]{:S(2)}, u32[]{:S(2)}) %collective-permute-start.6) | collective-permute-done | bytes 262176 | tf_op jit(solution)/shard_map/ppermute | solution.py:86
  137.2 22.3 %collective-permute-done.8 = bf16[256,512]{0,1:T(8,128)(2,1)S(1)} collective-permute-done((bf16[256,512]{0,1:T(8,128)(2,1)S(1)}, bf16[256,512]{0,1:T(8,128)(2,1)S(1)}, u32[]{:S(2)}, u32[]{:S(2)}) %collective-permute-start.8) | collective-permute-done | bytes 262176 | tf_op jit(solution)/shard_map/ppermute | solution.py:86
  159.7 22.7 %fusion.35 = (f32[2,16,256]{2,1,0:T(8,128)S(1)}, bf16[2,16,256,1152]{2,3,1,0:T(8,128)(2,1)}) fusion(pred[256,1152]{0,1:T(8,128)(4,1)S(1)} %compare_and_fusion, bf16[1152,2,128,1]{0,2,3,1:T(8,128)(2,1)S(1)} %bitcast.75, f32[256,2,16,64]{3,0,2,1:T(8,128)} %copy.19, f32[256,2,16,64]{3,0,2,1:T(8,128)} %copy.18, f32[256,2,16,128]{3,2,1,0:T(8,128)} %bitcast.71, ...), kind=kOutput, calls=%fused_computation.60 | convolution fusion | flops 2469397504 | bytes 28442624 | tf_op jit(solution)/shard_map/sub | solution.py:123
  182.4 9.3 %fusion.12 = bf16[256,2,16,128]{0,3,2,1:T(8,128)(2,1)S(1)} fusion(bf16[1152,2,128,1]{0,2,3,1:T(8,128)(2,1)S(1)} %bitcast.74, bf16[2,16,256,1152]{2,3,1,0:T(8,128)(2,1)} %get-tuple-element.14, f32[256,2,16]{0,2,1:T(8,128)S(1)} %bitcast.84), kind=kOutput, calls=%fused_computation.15 | convolution fusion | flops 2418016256 | bytes 21594112 | tf_op jit(solution)/shard_map/kgqn,nkd->kgqd/dot_general | solution.py:125
  191.7 2.9 %copy.22 = bf16[1,256,4096]{2,1,0:T(8,128)(2,1)} copy(bf16[1,256,4096]{1,2,0:T(8,128)(2,1)S(1)} %bitcast.72) | data formatting | bytes 4194304 | tf_op jit(solution)/shard_map/convert_element_type | solution.py:130
  (43 shorter events, 4.9 us)
Async XLA Ops:
  6.5 17.0 %copy-start.1 = (bf16[1,256,4096]{2,1,0:T(8,128)(2,1)S(1)}, bf16[1,256,4096]{2,1,0:T(8,128)(2,1)}, u32[]{:S(2)}) copy-start(bf16[1,256,4096]{2,1,0:T(8,128)(2,1)} %param.6) | copy-start | bytes 6291460
  6.5 97.5 %all-gather.2.cloned.1.call-start = ((), (), s32[]{:S(2)}) async-start(), calls=%async_computation | async-start | bytes 8912896 | tf_op jit(solution)/shard_map/all_gather | solution.py:59
  8.6 30.6 %collective-permute-start.3 = (s32[2]{0:T(128)}, s32[2]{0:T(128)S(1)}, u32[]{:S(2)}, u32[]{:S(2)}) collective-permute-start(s32[2]{0:T(128)} %bitcast.76), channel_id=1, source_target_pairs={{0,2},{2,4},{4,6},{6,8},{8,10},{10,12},{12,14},{1,3},{3,5},{5,7},{... | collective-permute-start | bytes 32 | tf_op jit(solution)/shard_map/ppermute | solution.py:87
  13.6 25.6 %collective-permute-start.2 = (s32[2]{0:T(128)}, s32[2]{0:T(128)S(1)}, u32[]{:S(2)}, u32[]{:S(2)}) collective-permute-start(s32[2]{0:T(128)} %bitcast.77), channel_id=1, source_target_pairs={{0,4},{2,6},{4,8},{6,10},{8,12},{10,14},{1,5},{3,7},{5,9},{7,11},{... | collective-permute-start | bytes 32 | tf_op jit(solution)/shard_map/ppermute | solution.py:87
  17.0 22.2 %collective-permute-start.1 = (s32[2]{0:T(128)}, s32[2]{0:T(128)S(1)}, u32[]{:S(2)}, u32[]{:S(2)}) collective-permute-start(s32[2]{0:T(128)} %bitcast.78), channel_id=1, source_target_pairs={{0,6},{2,8},{4,10},{6,12},{8,14},{1,7},{3,9},{5,11},{7,13},{9,15},... | collective-permute-start | bytes 32 | tf_op jit(solution)/shard_map/ppermute | solution.py:87
  20.2 19.0 %collective-permute-start = (s32[1]{0:T(128)}, s32[1]{0:T(128)}, u32[]{:S(2)}, u32[]{:S(2)}) collective-permute-start(s32[1]{0:T(128)} %bitcast), channel_id=1, source_target_pairs={{0,8},{2,10},{4,12},{6,14},{1,9},{3,11},{5,13},{7,15},{16,24},{18,... | collective-permute-start | bytes 20 | tf_op jit(solution)/shard_map/ppermute | solution.py:87
  22.0 86.2 %collective-permute-start.4 = (bf16[256,4096]{1,0:T(8,128)(2,1)}, bf16[256,4096]{1,0:T(8,128)(2,1)}, u32[]{:S(2)}, u32[]{:S(2)}) collective-permute-start(bf16[256,4096]{1,0:T(8,128)(2,1)} %bitcast.83), channel_id=1, source_target_pairs={{0,1},{1,0},{2,3},{3,2},{4,5},{5,4},{6,7},{7,6},{8,9},{9,8},{10,11... | collective-permute-start | bytes 6291464 | tf_op jit(solution)/shard_map/ppermute | solution.py:61
  27.0 3.7 %copy-start = (f32[1,256,4096]{1,2,0:T(8,128)S(1)}, f32[1,256,4096]{1,2,0:T(8,128)}, u32[]{:S(2)}) copy-start(f32[1,256,4096]{1,2,0:T(8,128)} %copy.17) | copy-start | bytes 12582916
  36.3 2.9 %copy-start.2 = (s32[1,2]{1,0:T(1,128)S(1)}, s32[1,2]{1,0:T(1,128)}, u32[]{:S(2)}) copy-start(s32[1,2]{1,0:T(1,128)} %param.9) | copy-start | bytes 28
  112.6 24.6 %collective-permute-start.7 = (bf16[256,512]{0,1:T(8,128)(2,1)S(1)}, bf16[256,512]{0,1:T(8,128)(2,1)S(1)}, u32[]{:S(2)}, u32[]{:S(2)}) collective-permute-start(bf16[256,512]{0,1:T(8,128)(2,1)S(1)} %pad_maximum_fusion.1), channel_id=1, source_target_pairs={{0,4},{2,6},{4,8},{6,10},{8,12},{10,14},{1,5},{3,7},{5,9},{7,11},{... | collective-permute-start | bytes 786440 | tf_op jit(solution)/shard_map/ppermute | solution.py:86
  118.0 18.2 %collective-permute-start.6 = (bf16[256,512]{0,1:T(8,128)(2,1)S(1)}, bf16[256,512]{0,1:T(8,128)(2,1)S(1)}, u32[]{:S(2)}, u32[]{:S(2)}) collective-permute-start(bf16[256,512]{0,1:T(8,128)(2,1)S(1)} %pad_maximum_fusion.1), channel_id=1, source_target_pairs={{0,6},{2,8},{4,10},{6,12},{8,14},{1,7},{3,9},{5,11},{7,13},{9,15},... | collective-permute-start | bytes 786440 | tf_op jit(solution)/shard_map/ppermute | solution.py:86
  120.0 5.1 %collective-permute-start.5 = (bf16[128,512]{0,1:T(8,128)(2,1)S(1)}, bf16[128,512]{0,1:T(8,128)(2,1)S(1)}, u32[]{:S(2)}, u32[]{:S(2)}) collective-permute-start(bf16[128,512]{0,1:T(8,128)(2,1)S(1)} %fusion.28), channel_id=1, source_target_pairs={{0,8},{2,10},{4,12},{6,14},{1,9},{3,11},{5,13},{7,15},{16,24},{18,... | collective-permute-start | bytes 393224 | tf_op jit(solution)/shard_map/ppermute | solution.py:86
  122.3 37.2 %collective-permute-start.8 = (bf16[256,512]{0,1:T(8,128)(2,1)S(1)}, bf16[256,512]{0,1:T(8,128)(2,1)S(1)}, u32[]{:S(2)}, u32[]{:S(2)}) collective-permute-start(bf16[256,512]{0,1:T(8,128)(2,1)S(1)} %pad_maximum_fusion.1), channel_id=1, source_target_pairs={{0,2},{2,4},{4,6},{6,8},{8,10},{10,12},{12,14},{1,3},{3,5},{5,7},{... | collective-permute-start | bytes 786440 | tf_op jit(solution)/shard_map/ppermute | solution.py:86
Sparse Core Ops, SparseCore 0:
  9.2 94.7 all-gather.1

commit v2 on v1

--- a/solution.py
+++ b/solution.py
@@ -3,6 +3,8 @@
 import jax
 import jax.numpy as jnp
 from jax import lax
+from jax.experimental import pallas as pl
+from jax.experimental.pallas import tpu as pltpu
 from jax.sharding import PartitionSpec as P
 
 HD = 128
@@ -42,6 +44,81 @@
     return vectors * cosine[:, None, :] + turned * sine_table[:, None, :]
 
 
+def flash_kernel(lo_ref, q_ref, k_ref, v_ref, o_ref, qs_ref, m_ref, l_ref, acc_ref):
+    qb = pl.program_id(0)
+    rows = o_ref.shape[0]
+    group = o_ref.shape[1] // HD
+    for g in range(group):
+        qs_ref[g * rows:(g + 1) * rows, :] = q_ref[:, g * HD:(g + 1) * HD]
+    m_ref[...] = jnp.full(m_ref.shape, MASKED_SCORE, jnp.float32)
+    l_ref[...] = jnp.zeros(l_ref.shape, jnp.float32)
+    acc_ref[...] = jnp.zeros(acc_ref.shape, jnp.float32)
+    own = LOOKBACK + qb
+    col = lax.broadcasted_iota(jnp.int32, (group, rows, BLOCK), 2)
+    row = lax.broadcasted_iota(jnp.int32, (group, rows, BLOCK), 1)
+
+    def step(j, carry):
+        start = pl.multiple_of(j * BLOCK, BLOCK)
+        keys = k_ref[pl.ds(start, BLOCK), :]
+        values = v_ref[pl.ds(start, BLOCK), :]
+        scores = lax.dot_general(
+            qs_ref[...], keys, (((1,), (1,)), ((), ())), preferred_element_type=jnp.float32
+        )
+        keep = col <= row + (own - j) * BLOCK
+        scores = jnp.where(keep, scores.reshape(group, rows, BLOCK), MASKED_SCORE)
+        scores = scores.reshape(group * rows, BLOCK)
+        m_old = m_ref[...]
+        m_new = jnp.maximum(m_old, jnp.max(scores, axis=1, keepdims=True))
+        alpha = jnp.exp(m_old - m_new)
+        probs = jnp.exp(scores - m_new)
+        l_ref[...] = alpha * l_ref[...] + jnp.sum(probs, axis=1, keepdims=True)
+        acc_ref[...] = alpha * acc_ref[...] + jnp.dot(
+            probs.astype(jnp.bfloat16), values, preferred_element_type=jnp.float32
+        )
+        m_ref[...] = m_new
+        return carry
+
+    lax.fori_loop(lo_ref[qb], own + 1, step, 0)
+    result = acc_ref[...] / l_ref[...]
+    for g in range(group):
+        o_ref[:, g * HD:(g + 1) * HD] = result[g * rows:(g + 1) * rows].astype(o_ref.dtype)
+
+
+def flash_attention(lo, query_rot, kv_all, kv_heads):
+    row_count, width = query_rot.shape
+    height = kv_all.shape[0]
+    q_blocks = row_count // BLOCK
+    group_width = width // kv_heads
+    group = group_width // HD
+    grid_spec = pltpu.PrefetchScalarGridSpec(
+        num_scalar_prefetch=1,
+        grid=(q_blocks, kv_heads),
+        in_specs=[
+            pl.BlockSpec((BLOCK, group_width), lambda qb, h, lo: (qb, h)),
+            pl.BlockSpec((height, HD), lambda qb, h, lo: (0, h)),
+            pl.BlockSpec((height, HD), lambda qb, h, lo: (0, kv_heads + h)),
+        ],
+        out_specs=pl.BlockSpec((BLOCK, group_width), lambda qb, h, lo: (qb, h)),
+        scratch_shapes=[
+            pltpu.VMEM((group * BLOCK, HD), jnp.bfloat16),
+            pltpu.VMEM((group * BLOCK, 1), jnp.float32),
+            pltpu.VMEM((group * BLOCK, 1), jnp.float32),
+            pltpu.VMEM((group * BLOCK, HD), jnp.float32),
+        ],
+    )
+    visits = q_blocks * kv_heads * (LOOKBACK + 1) // 2
+    return pl.pallas_call(
+        flash_kernel,
+        grid_spec=grid_spec,
+        out_shape=jax.ShapeDtypeStruct((row_count, width), jnp.bfloat16),
+        cost_estimate=pl.CostEstimate(
+            flops=visits * 4 * group * BLOCK * BLOCK * HD,
+            transcendentals=visits * group * BLOCK * BLOCK,
+            bytes_accessed=4 * row_count * width + 2 * kv_all.size,
+        ),
+    )(lo, query_rot, kv_all, kv_all)
+
+
 def shift_pairs(count, step):
     return [(i, i + step) for i in range(count - step)]
 
@@ -76,6 +153,7 @@
 
         local_docs = doc_blocks[0]
         blocks_here = row_count // BLOCK
+        doc_rows = jnp.zeros((16, 2 * kv_width), jnp.bfloat16)
         window_kv = []
         window_docs = []
         need = LOOKBACK
@@ -83,20 +161,30 @@
         while need > 0:
             take = min(need, blocks_here)
             pairs = shift_pairs(n_ctx, step)
-            window_kv.insert(0, lax.ppermute(kv_rows[(blocks_here - take) * BLOCK:], "ctx", pairs))
-            window_docs.insert(0, lax.ppermute(local_docs[blocks_here - take:], "ctx", pairs))
+            tagged = doc_rows.at[0, :take].set(local_docs[blocks_here - take:].astype(jnp.bfloat16))
+            payload = jnp.concatenate([kv_rows[(blocks_here - take) * BLOCK:], tagged], axis=0)
+            arrived = lax.ppermute(payload, "ctx", pairs)
+            window_kv.insert(0, arrived[:take * BLOCK])
+            window_docs.insert(0, arrived[take * BLOCK, :take].astype(jnp.int32))
             need -= take
             step += 1
         window_kv.append(kv_rows)
         window_docs.append(local_docs)
         kv_all = jnp.concatenate(window_kv, axis=0)
-        key_docs = jnp.repeat(jnp.concatenate(window_docs, axis=0), BLOCK)
-        height = kv_all.shape[0]
-        key_pos = ctx_rank * row_count - (height - row_count) + jnp.arange(height, dtype=jnp.int32)
+        block_docs = jnp.concatenate(window_docs, axis=0)
+        window_blocks = block_docs.shape[0]
+        block_index = jnp.arange(window_blocks, dtype=jnp.int32)
+        block_valid = ctx_rank * blocks_here - LOOKBACK + block_index >= 0
+        own = LOOKBACK + jnp.arange(blocks_here, dtype=jnp.int32)
+        same = (
+            block_valid[None, :]
+            & (block_docs[None, :] == local_docs[:, None])
+            & (block_index[None, :] <= own[:, None])
+        )
+        lo = own + 1 - jnp.sum(same.astype(jnp.int32), axis=1)
 
         local_queries = queries[0]
         query_heads = local_queries.shape[1] // HD
-        group_size = query_heads // kv_heads
         query_rot = (
             (
                 rotate(
@@ -106,29 +194,10 @@
                 )
                 * (ATTN_FACTOR / math.sqrt(HD))
             )
+            .reshape(row_count, query_heads * HD)
             .astype(jnp.bfloat16)
-            .reshape(row_count, kv_heads, group_size, HD)
-        )
-        query_docs = jnp.repeat(local_docs, BLOCK)
-        visible = (
-            (key_pos[None, :] <= positions[:, None])
-            & (key_pos[None, :] >= 0)
-            & (key_docs[None, :] == query_docs[:, None])
-        )
-        keys = kv_all[:, :kv_width].reshape(height, kv_heads, HD)
-        values = kv_all[:, kv_width:].reshape(height, kv_heads, HD)
-        scores = jnp.einsum("qkgd,nkd->kgqn", query_rot, keys, preferred_element_type=jnp.float32)
-        scores = jnp.where(visible, scores, MASKED_SCORE)
-        row_max = jnp.max(scores, axis=-1)
-        probs = jnp.where(visible, jnp.exp(scores - row_max[..., None]), 0.0)
-        row_sum = jnp.sum(probs, axis=-1)
-        mixed = jnp.einsum(
-            "kgqn,nkd->kgqd", probs.astype(jnp.bfloat16), values, preferred_element_type=jnp.float32
-        )
-        attended = mixed / row_sum[..., None]
-        context = (
-            attended.transpose(2, 0, 1, 3).reshape(row_count, query_heads * HD).astype(jnp.bfloat16)
-        )
+        )
+        context = flash_attention(lo, query_rot, kv_all, kv_heads)
         return context[None]
 
     return body

time: 202 us -> 238 us (1.18)
  the two profiles are of different devices: /device:TPU:100 before, /device:TPU:106 now
where the time goes in v2:
time: 238 us; the launch traced here: 234 us
  waiting for transfers between devices  97.7 us (41%)
  Pallas kernels  71.6 us (30%)
  other arithmetic  23.5 us (10%)
  between operations  14.3 us (6%)
  starting transfers between devices  13.5 us (6%)
  matrix products  7.57 us (3%)
  local copies, waits for them, and re-layouts  6.05 us (3%)
    pallas_call x1, Pallas kernels, flash_attention(): pl.pallas_call(flash_kernel, grid_spec=grid_spec, out_shape=jax.ShapeDtyp...  71.6 us
    all_gather x1, waiting for transfers between devices, body(): weights = lax.all_gather(joined, 'dp', axis=0, tiled=True)  60.4 us
    ppermute x4, waiting for transfers between devices, body(): arrived = lax.ppermute(payload, 'ctx', pairs)  37.3 us
    ppermute x4, starting transfers between devices, body(): arrived = lax.ppermute(payload, 'ctx', pairs)  11.2 us
    convert_element_type x1, other arithmetic, body(): query_rot = (rotate(local_queries.astype(jnp.float32).reshape(row_count,...  9.81 us
    neg x2, other arithmetic, rotate(): turned = jnp.concatenate([-upper_half, lower_half], axis=-1)  5.25 us
  transfers between devices with their start and end apart: 6, of which 4 were waited for; matrix products, arithmetic and copies ran while one was open for 12% of the time, Pallas kernels for 0%

profile of v2, /device:TPU:106, one launch (start us, length us, event | category | flops | bytes accessed | tf_op | source)
XLA Modules:
  0.0 234.2 jit_solution(18320579201567424309)
XLA Ops:
  6.5 1.9 pad_maximum_fusion
  8.4 2.2 collective-permute-start
  10.6 0.7 convert.13
  11.3 0.6 slice.108
  11.9 2.1 convert_bitcast_fusion
  14.0 2.7 %copy.15 = f32[32,8,32,128]{3,2,1,0:T(8,128)} copy(f32[32,8,32,128]{3,1,2,0:T(8,128)S(1)} %convert_bitcast_fusion) | data formatting | bytes 8388608
  16.8 0.5 multiply_cosine_fusion
  17.3 4.9 %slice_negate_fusion = (f32[256,32,64]{2,1,0:T(8,128)S(1)}, f32[256,32,64]{2,1,0:T(8,128)S(1)}) fusion(f32[256,32,128]{2,1,0:T(8,128)} %bitcast.66), kind=kLoop, calls=%fused_computation.6 | loop fusion | flops 524288 | bytes 8388608 | tf_op jit(solution)/shard_map/neg | solution.py:43
  22.4 1.3 maximum_multiply_fusion
  24.0 1.3 copy-done
  25.3 9.8 %fusion.3.q_ref = bf16[256,4096]{1,0:T(8,128)(2,1)} fusion(bf16[1,256,4096]{2,1,0:T(8,128)(2,1)S(1)} %copy-done, f32[32,8,32,128]{3,2,1,0:T(8,128)S(1)} %bitcast.67, f32[32,8,32,128]{3,2,1,0:T(8,128)S(1)} %bitcast.68), kind=kLoop, calls=%fused_computation.5 | loop fusion | flops 5242880 | bytes 12582912 | tf_op jit(solution)/shard_map/convert_element_type | solution.py:198
  35.1 60.4 %all-gather.2.cloned.1.call-done = bf16[8192,512]{1,0:T(8,128)(2,1)} async-done(((bf16[512,512]{1,0:T(8,128)(2,1)}), bf16[8192,512]{1,0:T(8,128)(2,1)}) %all-gather.2.cloned.1.call-update) | async-done | bytes 8388624 | tf_op jit(solution)/shard_map/all_gather | solution.py:136
  95.4 3.5 %fusion.6 = f32[512,256]{0,1:T(8,128)S(1)} fusion(bf16[2,4096,512]{2,1,0:T(8,128)(2,1)} %bitcast.73, s32[]{:T(128)S(6)} %select_n.6, bf16[1,256,4096]{2,1,0:T(8,128)(2,1)S(1)} %copy-done.3), kind=kOutput, calls=%fused_computation.10 | convolution fusion | flops 1073741824 | bytes 6815748 | tf_op jit(solution)/shard_map/dot_general | solution.py:139
  98.9 4.1 %fusion.13 = f32[256,512]{1,0:T(8,128)S(1)} fusion(f32[512,256]{0,1:T(8,128)S(1)} %fusion.6, bf16[256,4096]{1,0:T(8,128)(2,1)} %collective-permute-done, bf16[2,4096,512]{2,1,0:T(8,128)(2,1)} %bitcast.74, s32[]{:T(128)S(6)} %select_n.7), kind=kOutput, calls=%fused_computation.15 | convolution fusion | flops 1073872896 | bytes 7340036 | tf_op jit(solution)/shard_map/dot_general | solution.py:140
  104.1 0.6 fusion.21
  104.8 5.5 %collective-permute-start.1 = (bf16[144,512]{1,0:T(8,128)(2,1)S(1)}, bf16[144,512]{1,0:T(8,128)(2,1)S(1)}, u32[]{:S(2)}, u32[]{:S(2)}) collective-permute-start(bf16[144,512]{1,0:T(8,128)(2,1)S(1)} %fusion.21), channel_id=1, source_target_pairs={{0,8},{2,10},{4,12},{6,14},{1,9},{3,11},{5,13},{7,15},{16,24},{18,... | collective-permute-start | bytes 442376 | tf_op jit(solution)/shard_map/ppermute | solution.py:166
  110.3 1.9 collective-permute-start.2
  112.2 1.9 collective-permute-start.3
  114.2 1.9 collective-permute-start.4
  117.3 6.3 %collective-permute-done.2 = bf16[272,512]{1,0:T(8,128)(2,1)S(1)} collective-permute-done((bf16[272,512]{1,0:T(8,128)(2,1)S(1)}, bf16[272,512]{1,0:T(8,128)(2,1)S(1)}, u32[]{:S(2)}, u32[]{:S(2)}) %collective-permute-start.2) | collective-permute-done | bytes 278560 | tf_op jit(solution)/shard_map/ppermute | solution.py:166
  123.6 17.3 %collective-permute-done.3 = bf16[272,512]{1,0:T(8,128)(2,1)S(1)} collective-permute-done((bf16[272,512]{1,0:T(8,128)(2,1)S(1)}, bf16[272,512]{1,0:T(8,128)(2,1)S(1)}, u32[]{:S(2)}, u32[]{:S(2)}) %collective-permute-start.3) | collective-permute-done | bytes 278560 | tf_op jit(solution)/shard_map/ppermute | solution.py:166
  140.9 13.8 %collective-permute-done.4 = bf16[272,512]{1,0:T(8,128)(2,1)S(1)} collective-permute-done((bf16[272,512]{1,0:T(8,128)(2,1)S(1)}, bf16[272,512]{1,0:T(8,128)(2,1)S(1)}, u32[]{:S(2)}, u32[]{:S(2)}) %collective-permute-start.4) | collective-permute-done | bytes 278560 | tf_op jit(solution)/shard_map/ppermute | solution.py:166
  155.1 0.5 add_subtract_fusion.lo_ref
  155.8 71.6 %shard_map.55 = bf16[256,4096]{1,0:T(8,128)(2,1)} custom-call(s32[2]{0:T(128)} %add_subtract_fusion.lo_ref, bf16[256,4096]{1,0:T(8,128)(2,1)} %fusion.3.q_ref, bf16[1152,512]{1,0:T(8,128)(2,1)} %copy-done.1, bf16[1152,512]{1,0:T(8,128)(2,1)} %copy-done.1), custom_call_target="tpu_custom_call" | custom-call | flops 2147483648 | bytes 5373952 | tf_op jit(solution)/shard_map/pallas_call | solution.py:110
  (37 shorter events, 2.6 us)
Async XLA Ops:
  6.5 88.9 %all-gather.2.cloned.1.call-start = ((), (), s32[]{:S(2)}) async-start(), calls=%async_computation | async-start | bytes 8912896 | tf_op jit(solution)/shard_map/all_gather | solution.py:136
  8.4 90.5 %collective-permute-start = (bf16[256,4096]{1,0:T(8,128)(2,1)}, bf16[256,4096]{1,0:T(8,128)(2,1)}, u32[]{:S(2)}, u32[]{:S(2)}) collective-permute-start(bf16[256,4096]{1,0:T(8,128)(2,1)} %bitcast.75), channel_id=1, source_target_pairs={{0,1},{1,0},{2,3},{3,2},{4,5},{5,4},{6,7},{7,6},{8,9},{9,8},{10,11... | collective-permute-start | bytes 6291464 | tf_op jit(solution)/shard_map/ppermute | solution.py:138
  23.7 1.6 copy-start
  25.3 70.2 %copy-start.3 = (bf16[1,256,4096]{2,1,0:T(8,128)(2,1)S(1)}, bf16[1,256,4096]{2,1,0:T(8,128)(2,1)}, u32[]{:S(2)}) copy-start(bf16[1,256,4096]{2,1,0:T(8,128)(2,1)} %param.13) | copy-start | bytes 6291460
  103.0 51.8 %copy-start.2 = (s32[1,2]{1,0:T(1,128)S(1)}, s32[1,2]{1,0:T(1,128)}, u32[]{:S(2)}) copy-start(s32[1,2]{1,0:T(1,128)} %param.17) | copy-start | bytes 28
  104.8 11.3 %collective-permute-start.1 = (bf16[144,512]{1,0:T(8,128)(2,1)S(1)}, bf16[144,512]{1,0:T(8,128)(2,1)S(1)}, u32[]{:S(2)}, u32[]{:S(2)}) collective-permute-start(bf16[144,512]{1,0:T(8,128)(2,1)S(1)} %fusion.21), channel_id=1, source_target_pairs={{0,8},{2,10},{4,12},{6,14},{1,9},{3,11},{5,13},{7,15},{16,24},{18,... | collective-permute-start | bytes 442376 | tf_op jit(solution)/shard_map/ppermute | solution.py:166
  110.3 13.3 %collective-permute-start.2 = (bf16[272,512]{1,0:T(8,128)(2,1)S(1)}, bf16[272,512]{1,0:T(8,128)(2,1)S(1)}, u32[]{:S(2)}, u32[]{:S(2)}) collective-permute-start(bf16[272,512]{1,0:T(8,128)(2,1)S(1)} %fusion.18), channel_id=1, source_target_pairs={{0,6},{2,8},{4,10},{6,12},{8,14},{1,7},{3,9},{5,11},{7,13},{9,15},... | collective-permute-start | bytes 835592 | tf_op jit(solution)/shard_map/ppermute | solution.py:166
  112.2 28.7 %collective-permute-start.3 = (bf16[272,512]{1,0:T(8,128)(2,1)S(1)}, bf16[272,512]{1,0:T(8,128)(2,1)S(1)}, u32[]{:S(2)}, u32[]{:S(2)}) collective-permute-start(bf16[272,512]{1,0:T(8,128)(2,1)S(1)} %fusion.18), channel_id=1, source_target_pairs={{0,4},{2,6},{4,8},{6,10},{8,12},{10,14},{1,5},{3,7},{5,9},{7,11},{... | collective-permute-start | bytes 835592 | tf_op jit(solution)/shard_map/ppermute | solution.py:166
  114.2 40.5 %collective-permute-start.4 = (bf16[272,512]{1,0:T(8,128)(2,1)S(1)}, bf16[272,512]{1,0:T(8,128)(2,1)S(1)}, u32[]{:S(2)}, u32[]{:S(2)}) collective-permute-start(bf16[272,512]{1,0:T(8,128)(2,1)S(1)} %fusion.18), channel_id=1, source_target_pairs={{0,2},{2,4},{4,6},{6,8},{8,10},{10,12},{12,14},{1,3},{3,5},{5,7},{... | collective-permute-start | bytes 835592 | tf_op jit(solution)/shard_map/ppermute | solution.py:166
  154.7 1.0 copy-start.1
Sparse Core Ops, SparseCore 0:
  9.2 86.2 all-gather.1

commit v3 on v1

--- a/solution.py
+++ b/solution.py
@@ -3,6 +3,8 @@
 import jax
 import jax.numpy as jnp
 from jax import lax
+from jax.experimental import pallas as pl
+from jax.experimental.pallas import tpu as pltpu
 from jax.sharding import PartitionSpec as P
 
 HD = 128
@@ -42,6 +44,63 @@
     return vectors * cosine[:, None, :] + turned * sine_table[:, None, :]
 
 
+def dense_kernel(vis_ref, q_ref, k_ref, v_ref, o_ref, qs_ref):
+    rows = o_ref.shape[0]
+    group = o_ref.shape[1] // HD
+    for g in range(group):
+        qs_ref[g * rows:(g + 1) * rows, :] = q_ref[:, g * HD:(g + 1) * HD]
+    visible = vis_ref[...] != 0
+    keys = k_ref[...]
+    values = v_ref[...]
+    height = keys.shape[0]
+    part = group // 2
+    for half in range(2):
+        stacked = qs_ref[half * part * rows:(half + 1) * part * rows, :]
+        scores = lax.dot_general(
+            stacked, keys, (((1,), (1,)), ((), ())), preferred_element_type=jnp.float32
+        )
+        scores = jnp.where(visible[None], scores.reshape(part, rows, height), MASKED_SCORE)
+        row_max = jnp.max(scores, axis=2, keepdims=True)
+        probs = jnp.where(visible[None], jnp.exp(scores - row_max), 0.0)
+        row_sum = jnp.sum(probs, axis=2, keepdims=True)
+        mixed = jnp.dot(
+            probs.reshape(part * rows, height).astype(jnp.bfloat16),
+            values,
+            preferred_element_type=jnp.float32,
+        )
+        result = mixed.reshape(part, rows, HD) / row_sum
+        for g in range(part):
+            head = half * part + g
+            o_ref[:, head * HD:(head + 1) * HD] = result[g].astype(o_ref.dtype)
+
+
+def dense_attention(visible, query_rot, kv_all, kv_heads):
+    row_count, width = query_rot.shape
+    height = kv_all.shape[0]
+    q_blocks = row_count // BLOCK
+    group_width = width // kv_heads
+    group = group_width // HD
+    return pl.pallas_call(
+        dense_kernel,
+        grid=(q_blocks, kv_heads),
+        in_specs=[
+            pl.BlockSpec((BLOCK, height), lambda qb, h: (qb, 0)),
+            pl.BlockSpec((BLOCK, group_width), lambda qb, h: (qb, h)),
+            pl.BlockSpec((height, HD), lambda qb, h: (0, h)),
+            pl.BlockSpec((height, HD), lambda qb, h: (0, kv_heads + h)),
+        ],
+        out_specs=pl.BlockSpec((BLOCK, group_width), lambda qb, h: (qb, h)),
+        scratch_shapes=[pltpu.VMEM((group * BLOCK, HD), jnp.bfloat16)],
+        out_shape=jax.ShapeDtypeStruct((row_count, width), jnp.bfloat16),
+        compiler_params=pltpu.CompilerParams(vmem_limit_bytes=48 * 1024 * 1024),
+        cost_estimate=pl.CostEstimate(
+            flops=4 * row_count * width * height,
+            transcendentals=row_count * (width // HD) * height,
+            bytes_accessed=4 * row_count * width + 2 * kv_all.size + 4 * row_count * height,
+        ),
+    )(visible, query_rot, kv_all, kv_all)
+
+
 def shift_pairs(count, step):
     return [(i, i + step) for i in range(count - step)]
 
@@ -76,6 +135,7 @@
 
         local_docs = doc_blocks[0]
         blocks_here = row_count // BLOCK
+        doc_rows = jnp.zeros((16, 2 * kv_width), jnp.bfloat16)
         window_kv = []
         window_docs = []
         need = LOOKBACK
@@ -83,20 +143,29 @@
         while need > 0:
             take = min(need, blocks_here)
             pairs = shift_pairs(n_ctx, step)
-            window_kv.insert(0, lax.ppermute(kv_rows[(blocks_here - take) * BLOCK:], "ctx", pairs))
-            window_docs.insert(0, lax.ppermute(local_docs[blocks_here - take:], "ctx", pairs))
+            tagged = doc_rows.at[0, :take].set(local_docs[blocks_here - take:].astype(jnp.bfloat16))
+            payload = jnp.concatenate([kv_rows[(blocks_here - take) * BLOCK:], tagged], axis=0)
+            arrived = lax.ppermute(payload, "ctx", pairs)
+            window_kv.insert(0, arrived[:take * BLOCK])
+            window_docs.insert(0, arrived[take * BLOCK, :take].astype(jnp.int32))
             need -= take
             step += 1
         window_kv.append(kv_rows)
         window_docs.append(local_docs)
         kv_all = jnp.concatenate(window_kv, axis=0)
-        key_docs = jnp.repeat(jnp.concatenate(window_docs, axis=0), BLOCK)
+        block_docs = jnp.concatenate(window_docs, axis=0)
         height = kv_all.shape[0]
         key_pos = ctx_rank * row_count - (height - row_count) + jnp.arange(height, dtype=jnp.int32)
+        key_docs = jnp.repeat(block_docs, BLOCK)
+        query_docs = jnp.repeat(local_docs, BLOCK)
+        visible = (
+            (key_pos[None, :] <= positions[:, None])
+            & (key_pos[None, :] >= 0)
+            & (key_docs[None, :] == query_docs[:, None])
+        ).astype(jnp.int32)
 
         local_queries = queries[0]
         query_heads = local_queries.shape[1] // HD
-        group_size = query_heads // kv_heads
         query_rot = (
             (
                 rotate(
@@ -106,29 +175,10 @@
                 )
                 * (ATTN_FACTOR / math.sqrt(HD))
             )
+            .reshape(row_count, query_heads * HD)
             .astype(jnp.bfloat16)
-            .reshape(row_count, kv_heads, group_size, HD)
-        )
-        query_docs = jnp.repeat(local_docs, BLOCK)
-        visible = (
-            (key_pos[None, :] <= positions[:, None])
-            & (key_pos[None, :] >= 0)
-            & (key_docs[None, :] == query_docs[:, None])
-        )
-        keys = kv_all[:, :kv_width].reshape(height, kv_heads, HD)
-        values = kv_all[:, kv_width:].reshape(height, kv_heads, HD)
-        scores = jnp.einsum("qkgd,nkd->kgqn", query_rot, keys, preferred_element_type=jnp.float32)
-        scores = jnp.where(visible, scores, MASKED_SCORE)
-        row_max = jnp.max(scores, axis=-1)
-        probs = jnp.where(visible, jnp.exp(scores - row_max[..., None]), 0.0)
-        row_sum = jnp.sum(probs, axis=-1)
-        mixed = jnp.einsum(
-            "kgqn,nkd->kgqd", probs.astype(jnp.bfloat16), values, preferred_element_type=jnp.float32
-        )
-        attended = mixed / row_sum[..., None]
-        context = (
-            attended.transpose(2, 0, 1, 3).reshape(row_count, query_heads * HD).astype(jnp.bfloat16)
-        )
+        )
+        context = dense_attention(visible, query_rot, kv_all, kv_heads)
         return context[None]
 
     return body

time: 202 us -> 192 us (0.950)
  matrix products: 40.3 us -> 8.13 us
  Pallas kernels: 0 us -> 24.3 us
  other arithmetic: 6.23 us -> 22.6 us
  local copies, waits for them, and re-layouts: 18.7 us -> 7.3 us
  starting transfers between devices: 24 us -> 12.8 us
  waiting for transfers between devices: 98.4 us -> 101 us
    pallas_call x0 -> x1, Pallas kernels: none -> 24.3 us  [dense_attention(): pl.pallas_call(dense_kernel, grid=(q_blocks, kv_heads), in_specs=[pl.Bloc...]
    sub x1 -> x0, matrix products: 22.7 us -> none  [body(): probs = jnp.where(visible, jnp.exp(scores - row_max[..., None]), 0.0)]
    ppermute x8 -> x4, starting transfers between devices: 23.5 us -> 12.2 us  [body(): arrived = lax.ppermute(payload, 'ctx', pairs)]
    dot_general x1 -> x0, matrix products: 9.26 us -> none  [body(): jnp.einsum('kgqn,nkd->kgqd', probs.astype(jnp.bfloat16), values, preferre...]
    convert_element_type x0 -> x5, other arithmetic: none -> 8.93 us  [the longest x1 8.62 us: body(): query_rot = (rotate(local_queries.astype(jnp.float32).reshape(row_count,...]
    concatenate x5 -> x1, local copies, waits for them, and re-layouts: 7.53 us -> 0.74 us  [body(): block_docs = jnp.concatenate(window_docs, axis=0)]
    convert_element_type x2 -> x0, local copies, waits for them, and re-layouts: 5.88 us -> none  [the longest x1 3.02 us: body(): local_queries.astype(jnp.float32).reshape(row_count, query_heads, HD)]
    neg x2, other arithmetic: 1.76 us -> 5.25 us  [rotate(): turned = jnp.concatenate([-upper_half, lower_half], axis=-1)]
  transfers between devices with their start and end apart: 10 -> 6, of which waited for: 4 -> 4; matrix products, arithmetic and copies ran while one was open for 11% -> 14% of each run, Pallas kernels for 0% -> 0%
where the time goes in v3:
time: 192 us; the launch traced here: 190 us
  waiting for transfers between devices  101 us (53%)
  Pallas kernels  24.3 us (13%)
  other arithmetic  22.6 us (12%)
  between operations  14.3 us (7%)
  starting transfers between devices  12.8 us (7%)
  matrix products  8.13 us (4%)
  local copies, waits for them, and re-layouts  7.3 us (4%)
    all_gather x1, waiting for transfers between devices, body(): weights = lax.all_gather(joined, 'dp', axis=0, tiled=True)  64.6 us
    ppermute x4, waiting for transfers between devices, body(): arrived = lax.ppermute(payload, 'ctx', pairs)  36.3 us
    pallas_call x1, Pallas kernels, dense_attention(): pl.pallas_call(dense_kernel, grid=(q_blocks, kv_heads), in_specs=[pl.Bloc...  24.3 us
    ppermute x4, starting transfers between devices, body(): arrived = lax.ppermute(payload, 'ctx', pairs)  12.2 us
    convert_element_type x1, other arithmetic, body(): query_rot = (rotate(local_queries.astype(jnp.float32).reshape(row_count,...  8.62 us
    neg x2, other arithmetic, rotate(): turned = jnp.concatenate([-upper_half, lower_half], axis=-1)  5.25 us
    unnamed x11, local copies, waits for them, and re-layouts  4.71 us
    dot_general x1, matrix products, body(): jnp.dot(partner_tokens, weights[1 - tp_rank], preferred_element_type=jnp....  4.07 us
  transfers between devices with their start and end apart: 6, of which 4 were waited for; matrix products, arithmetic and copies ran while one was open for 14% of the time, Pallas kernels for 0%

profile of v3, /device:TPU:100, one launch (start us, length us, event | category | flops | bytes accessed | tf_op | source)
XLA Modules:
  0.0 190.3 jit_solution(3318868889145386177)
XLA Ops:
  6.5 1.9 pad_maximum_fusion
  8.4 0.6 collective-permute-start
  9.0 0.7 convert.13
  10.3 0.7 slice.108
  10.9 2.1 %convert_bitcast_fusion = f32[32,8,32,128]{3,1,2,0:T(8,128)S(1)} fusion(bf16[1,256,4096]{2,1,0:T(8,128)(2,1)} %param.14), kind=kLoop, calls=%fused_computation | loop fusion | flops 1048576 | bytes 6291456
  13.0 2.7 %copy.13 = f32[32,8,32,128]{3,2,1,0:T(8,128)} copy(f32[32,8,32,128]{3,1,2,0:T(8,128)S(1)} %convert_bitcast_fusion) | data formatting | bytes 8388608
  16.4 4.9 %slice_negate_fusion = (f32[256,32,64]{2,1,0:T(8,128)S(1)}, f32[256,32,64]{2,1,0:T(8,128)S(1)}) fusion(f32[256,32,128]{2,1,0:T(8,128)} %bitcast.70), kind=kLoop, calls=%fused_computation.6 | loop fusion | flops 524288 | bytes 8388608 | tf_op jit(solution)/shard_map/neg | solution.py:43
  21.5 1.3 maximum_multiply_fusion
  23.0 1.3 copy-done
  24.4 8.6 %fusion.3.q_ref = bf16[256,4096]{1,0:T(8,128)(2,1)S(1)} fusion(bf16[1,256,4096]{2,1,0:T(8,128)(2,1)S(1)} %copy-done, f32[32,8,32,128]{3,2,1,0:T(8,128)S(1)} %bitcast.71, f32[32,8,32,128]{3,2,1,0:T(8,128)S(1)} %bitcast.72), kind=kLoop, calls=%fused_computation.5 | loop fusion | flops 5242880 | bytes 12582912 | tf_op jit(solution)/shard_map/convert_element_type | solution.py:179
  33.0 64.6 %all-gather.2.cloned.1.call-done = bf16[8192,512]{1,0:T(8,128)(2,1)} async-done(((bf16[512,512]{1,0:T(8,128)(2,1)}), bf16[8192,512]{1,0:T(8,128)(2,1)}) %all-gather.2.cloned.1.call-update) | async-done | bytes 8388624 | tf_op jit(solution)/shard_map/all_gather | solution.py:118
  97.6 4.1 %fusion.6 = f32[512,256]{0,1:T(8,128)S(1)} fusion(bf16[2,4096,512]{2,1,0:T(8,128)(2,1)} %bitcast.77, s32[]{:T(128)S(6)} %select_n.6, bf16[1,256,4096]{2,1,0:T(8,128)(2,1)} %param.13), kind=kOutput, calls=%fused_computation.10 | convolution fusion | flops 1073741824 | bytes 6815748 | tf_op jit(solution)/shard_map/dot_general | solution.py:121
  101.7 4.1 %fusion.13 = f32[256,512]{1,0:T(8,128)S(1)} fusion(f32[512,256]{0,1:T(8,128)S(1)} %fusion.6, bf16[256,4096]{1,0:T(8,128)(2,1)} %collective-permute-done, bf16[2,4096,512]{2,1,0:T(8,128)(2,1)} %bitcast.78, s32[]{:T(128)S(6)} %select_n.7), kind=kOutput, calls=%fused_computation.15 | convolution fusion | flops 1073872896 | bytes 7340036 | tf_op jit(solution)/shard_map/dot_general | solution.py:122
  106.8 0.7 fusion.21
  107.6 6.4 %collective-permute-start.1 = (bf16[144,512]{1,0:T(8,128)(2,1)S(1)}, bf16[144,512]{1,0:T(8,128)(2,1)S(1)}, u32[]{:S(2)}, u32[]{:S(2)}) collective-permute-start(bf16[144,512]{1,0:T(8,128)(2,1)S(1)} %fusion.21), channel_id=1, source_target_pairs={{0,8},{2,10},{4,12},{6,14},{1,9},{3,11},{5,13},{7,15},{16,24},{18,... | collective-permute-start | bytes 442376 | tf_op jit(solution)/shard_map/ppermute | solution.py:148
  114.0 0.7 fusion.18
  114.7 1.9 %collective-permute-start.2 = (bf16[272,512]{1,0:T(8,128)(2,1)S(1)}, bf16[272,512]{1,0:T(8,128)(2,1)S(1)}, u32[]{:S(2)}, u32[]{:S(2)}) collective-permute-start(bf16[272,512]{1,0:T(8,128)(2,1)S(1)} %fusion.18), channel_id=1, source_target_pairs={{0,6},{2,8},{4,10},{6,12},{8,14},{1,7},{3,9},{5,11},{7,13},{9,15},... | collective-permute-start | bytes 835592 | tf_op jit(solution)/shard_map/ppermute | solution.py:148
  116.6 1.9 %collective-permute-start.3 = (bf16[272,512]{1,0:T(8,128)(2,1)S(1)}, bf16[272,512]{1,0:T(8,128)(2,1)S(1)}, u32[]{:S(2)}, u32[]{:S(2)}) collective-permute-start(bf16[272,512]{1,0:T(8,128)(2,1)S(1)} %fusion.18), channel_id=1, source_target_pairs={{0,4},{2,6},{4,8},{6,10},{8,12},{10,14},{1,5},{3,7},{5,9},{7,11},{... | collective-permute-start | bytes 835592 | tf_op jit(solution)/shard_map/ppermute | solution.py:148
  118.5 1.9 %collective-permute-start.4 = (bf16[272,512]{1,0:T(8,128)(2,1)S(1)}, bf16[272,512]{1,0:T(8,128)(2,1)S(1)}, u32[]{:S(2)}, u32[]{:S(2)}) collective-permute-start(bf16[272,512]{1,0:T(8,128)(2,1)S(1)} %fusion.18), channel_id=1, source_target_pairs={{0,2},{2,4},{4,6},{6,8},{8,10},{10,12},{12,14},{1,3},{3,5},{5,7},{... | collective-permute-start | bytes 835592 | tf_op jit(solution)/shard_map/ppermute | solution.py:148
  121.7 6.3 %collective-permute-done.2 = bf16[272,512]{1,0:T(8,128)(2,1)S(1)} collective-permute-done((bf16[272,512]{1,0:T(8,128)(2,1)S(1)}, bf16[272,512]{1,0:T(8,128)(2,1)S(1)}, u32[]{:S(2)}, u32[]{:S(2)}) %collective-permute-start.2) | collective-permute-done | bytes 278560 | tf_op jit(solution)/shard_map/ppermute | solution.py:148
  128.0 15.9 %collective-permute-done.3 = bf16[272,512]{1,0:T(8,128)(2,1)S(1)} collective-permute-done((bf16[272,512]{1,0:T(8,128)(2,1)S(1)}, bf16[272,512]{1,0:T(8,128)(2,1)S(1)}, u32[]{:S(2)}, u32[]{:S(2)}) %collective-permute-start.3) | collective-permute-done | bytes 278560 | tf_op jit(solution)/shard_map/ppermute | solution.py:148
  143.9 14.1 %collective-permute-done.4 = bf16[272,512]{1,0:T(8,128)(2,1)S(1)} collective-permute-done((bf16[272,512]{1,0:T(8,128)(2,1)S(1)}, bf16[272,512]{1,0:T(8,128)(2,1)S(1)}, u32[]{:S(2)}, u32[]{:S(2)}) %collective-permute-start.4) | collective-permute-done | bytes 278560 | tf_op jit(solution)/shard_map/ppermute | solution.py:148
  158.1 0.7 concatenate.45
  159.2 24.3 %shard_map.55 = bf16[256,4096]{1,0:T(8,128)(2,1)} custom-call(s32[256,1152]{1,0:T(8,128)S(1)} %and_convert_fusion.vis_ref, bf16[256,4096]{1,0:T(8,128)(2,1)S(1)} %fusion.3.q_ref, bf16[1152,512]{1,0:T(8,128)(2,1)S(1)} %fusion.19.k_ref.v_ref, bf16[1152,512]{1,0:T(8,128)(2,1)S(1)} %fusion.19.k_ref.v_ref), custom_call_target="tpu_custom_call" | custom-call | flops 4831838208 | bytes 6553600 | tf_op jit(solution)/shard_map/pallas_call | solution.py:83
  (37 shorter events, 3.7 us)
Async XLA Ops:
  6.5 91.1 %all-gather.2.cloned.1.call-start = ((), (), s32[]{:S(2)}) async-start(), calls=%async_computation | async-start | bytes 8912896 | tf_op jit(solution)/shard_map/all_gather | solution.py:118
  8.4 93.2 %collective-permute-start = (bf16[256,4096]{1,0:T(8,128)(2,1)}, bf16[256,4096]{1,0:T(8,128)(2,1)}, u32[]{:S(2)}, u32[]{:S(2)}) collective-permute-start(bf16[256,4096]{1,0:T(8,128)(2,1)} %bitcast.79), channel_id=1, source_target_pairs={{0,1},{1,0},{2,3},{3,2},{4,5},{5,4},{6,7},{7,6},{8,9},{9,8},{10,11... | collective-permute-start | bytes 6291464 | tf_op jit(solution)/shard_map/ppermute | solution.py:120
  9.7 0.6 copy-start.1
  16.4 4.9 %copy-start.2 = (s32[1,2]{1,0:T(1,128)S(1)}, s32[1,2]{1,0:T(1,128)}, u32[]{:S(2)}) copy-start(s32[1,2]{1,0:T(1,128)} %param.17) | copy-start | bytes 28
  22.7 1.6 copy-start
  107.6 12.9 %collective-permute-start.1 = (bf16[144,512]{1,0:T(8,128)(2,1)S(1)}, bf16[144,512]{1,0:T(8,128)(2,1)S(1)}, u32[]{:S(2)}, u32[]{:S(2)}) collective-permute-start(bf16[144,512]{1,0:T(8,128)(2,1)S(1)} %fusion.21), channel_id=1, source_target_pairs={{0,8},{2,10},{4,12},{6,14},{1,9},{3,11},{5,13},{7,15},{16,24},{18,... | collective-permute-start | bytes 442376 | tf_op jit(solution)/shard_map/ppermute | solution.py:148
  114.7 13.3 %collective-permute-start.2 = (bf16[272,512]{1,0:T(8,128)(2,1)S(1)}, bf16[272,512]{1,0:T(8,128)(2,1)S(1)}, u32[]{:S(2)}, u32[]{:S(2)}) collective-permute-start(bf16[272,512]{1,0:T(8,128)(2,1)S(1)} %fusion.18), channel_id=1, source_target_pairs={{0,6},{2,8},{4,10},{6,12},{8,14},{1,7},{3,9},{5,11},{7,13},{9,15},... | collective-permute-start | bytes 835592 | tf_op jit(solution)/shard_map/ppermute | solution.py:148
  116.6 27.3 %collective-permute-start.3 = (bf16[272,512]{1,0:T(8,128)(2,1)S(1)}, bf16[272,512]{1,0:T(8,128)(2,1)S(1)}, u32[]{:S(2)}, u32[]{:S(2)}) collective-permute-start(bf16[272,512]{1,0:T(8,128)(2,1)S(1)} %fusion.18), channel_id=1, source_target_pairs={{0,4},{2,6},{4,8},{6,10},{8,12},{10,14},{1,5},{3,7},{5,9},{7,11},{... | collective-permute-start | bytes 835592 | tf_op jit(solution)/shard_map/ppermute | solution.py:148
  118.5 39.5 %collective-permute-start.4 = (bf16[272,512]{1,0:T(8,128)(2,1)S(1)}, bf16[272,512]{1,0:T(8,128)(2,1)S(1)}, u32[]{:S(2)}, u32[]{:S(2)}) collective-permute-start(bf16[272,512]{1,0:T(8,128)(2,1)S(1)} %fusion.18), channel_id=1, source_target_pairs={{0,2},{2,4},{4,6},{6,8},{8,10},{10,12},{12,14},{1,3},{3,5},{5,7},{... | collective-permute-start | bytes 835592 | tf_op jit(solution)/shard_map/ppermute | solution.py:148
Sparse Core Ops, SparseCore 0:
  9.2 88.3 all-gather.1
